TPU v7x, 512 devices: a whole 4x4x16 slice. The times are simulated.
512 devices in a mesh: tensor: 32 (over z_hi, x, core), seq: 16 (over z_lo, y).
Axes of the slice: x: 4, y: 4, z: 16 (z_hi: 4, z_lo: 4; z = z_hi * 4 + z_lo), core: 2. Of those that a mesh axis runs over, the one named last changes fastest.
Arguments:
- resid: bfloat16 [16, 512, 2048], P('seq', 'tensor'), may hold values from -6 to 6
- norm_gain: bfloat16 [2048], replicated, may hold values from 0.099609375 to 1.8984375
- gate_weight_matrix: bfloat16 [2048, 10944], P(None, 'tensor'), may hold values from -0.125 to 0.125
- up_weight: bfloat16 [2048, 10944], P(None, 'tensor'), may hold values from -0.125 to 0.125
- w_down: bfloat16 [10944, 2048], P('tensor'), may hold values from -0.0546875 to 0.0546875
- gate_a: bfloat16 [64, 2048, 16], P('seq', 'tensor'), may hold values from -0.125 to 0.125
- gate_b: bfloat16 [64, 16, 10944], P('seq', None, 'tensor'), may hold values from -1.5 to 1.5
- up_a: bfloat16 [64, 2048, 16], P('seq', 'tensor'), may hold values from -0.125 to 0.125
- up_b: bfloat16 [64, 16, 10944], P('seq', None, 'tensor'), may hold values from -1.5 to 1.5
- down_a: bfloat16 [64, 10944, 16], P('seq', 'tensor'), may hold values from -0.0546875 to 0.0546875
- down_b: bfloat16 [64, 16, 2048], P('seq'), may hold values from -1.5 to 1.5
- prompt_lengths: int32 [16, 8], P('seq'), may hold values from 1 to 256, 512 in all within a row
- prompt_choice: int32 [16, 8], P('seq'), may hold values from 0 to 15
- used_adapters: int32 [16], replicated, may hold values from 0 to 63, as said below
- adapter_holder: int32 [64], replicated, may hold values from 0 to 63, each once
Outputs:
- output: bfloat16 [16, 512, 2048], P('seq', 'tensor')
Inputs may be any that keep to these rules, and one draw needn't show every extreme that they name: `used_adapters`: 16 distinct adapter ids.
All inputs are finite; a program needn't handle non-finite values.
Results may differ from a plain program's by a relative error of at most 0.017.
Values may be sent and summed in bfloat16 or wider, within the bound.
No kernel may reach another device: no remote copies, remote signals or barrier semaphores. Data moves between devices by JAX's collectives and lax.ppermute only.
A program may use at most 128 MiB of HBM per device.

v0:
```python
import jax
import jax.numpy as jnp
from jax import lax
from jax.sharding import PartitionSpec as P

adapter_scale = 0.5


def pick_rows(picker, stacked):
    flat = stacked.reshape(stacked.shape[0], -1)
    chosen = jnp.dot(picker, flat, preferred_element_type=jnp.float32).astype(jnp.bfloat16)
    return chosen.reshape((picker.shape[0],) + stacked.shape[1:])


def select_token(values, weights):
    return jnp.sum(values * weights[:, :, None], axis=1)


def local(
    resid,
    norm_gain,
    gate_weight_matrix,
    up_weight,
    w_down,
    gate_a,
    gate_b,
    up_a,
    up_b,
    down_a,
    down_b,
    prompt_lengths,
    prompt_choice,
    used_adapters,
    adapter_holder,
):
    tensor_n = lax.axis_size("tensor")
    tok_dev = resid.shape[1]
    d_model = resid.shape[2]
    group_tok = tok_dev * tensor_n
    used_n = used_adapters.shape[0]
    rank_n = gate_a.shape[2]
    feat_loc = gate_a.shape[1]
    slots_loc = gate_a.shape[0]
    hidden_local = gate_weight_matrix.shape[1]
    adapters_n = adapter_holder.shape[0]
    matches = used_adapters[:, None] == jnp.arange(adapters_n, dtype=jnp.int32)[None, :]
    slot_used = jnp.sum(jnp.where(matches, adapter_holder[None, :], 0), axis=1)
    picker = (slot_used[:, None] == jnp.arange(adapters_n, dtype=jnp.int32)[None, :]).astype(
        jnp.bfloat16
    )
    pieces = (gate_a, up_a, gate_b, up_b, down_a)
    widths = [p.shape[1] * p.shape[2] for p in pieces]
    pack = jnp.concatenate([p.reshape(slots_loc, -1) for p in pieces], axis=1)
    whole = lax.all_gather(pack, "seq", axis=0, tiled=True)
    chosen = pick_rows(picker, whole)
    offs = [0]
    for w in widths:
        offs.append(offs[-1] + w)
    sel = [
        chosen[:, offs[i] : offs[i + 1]].reshape((used_n,) + pieces[i].shape[1:])
        for i in range(len(pieces))
    ]
    sel_ga, sel_ua, sel_gb, sel_ub, sel_da = sel
    whole_db = lax.all_gather(down_b, "seq", axis=0, tiled=True)
    sel_db = pick_rows(picker, whole_db)
    prompt_ends = jnp.cumsum(prompt_lengths[0])
    positions = jnp.arange(group_tok, dtype=jnp.int32)
    prompt_index = jnp.sum((positions[:, None] >= prompt_ends[None, :]).astype(jnp.int32), axis=1)
    prompts_n = prompt_lengths.shape[1]
    hits = prompt_index[:, None] == jnp.arange(prompts_n, dtype=jnp.int32)[None, :]
    tok_choice = jnp.sum(jnp.where(hits, prompt_choice[0][None, :], 0), axis=1)
    token_weights = (tok_choice[:, None] == jnp.arange(used_n, dtype=jnp.int32)[None, :]).astype(
        jnp.float32
    )
    row_first = lax.axis_index("tensor") * tok_dev
    own_weights = lax.dynamic_slice_in_dim(token_weights, row_first, tok_dev, 0)
    residual_float = resid[0].astype(jnp.float32)
    scale = lax.rsqrt(jnp.mean(residual_float * residual_float, axis=-1, keepdims=True) + 1e-06)
    normalized_input = (residual_float * scale * norm_gain.astype(jnp.float32)).astype(jnp.bfloat16)
    tpack = jnp.concatenate(
        [normalized_input.reshape(-1), sel_ga.reshape(-1), sel_ua.reshape(-1)], axis=0
    )
    tall = lax.all_gather(tpack, "tensor", axis=0, tiled=False)
    n_tok_el = tok_dev * d_model
    n_a_el = used_n * feat_loc * rank_n
    piece = tall[:, :n_tok_el].reshape(group_tok, d_model)
    ga_all = tall[:, n_tok_el : n_tok_el + n_a_el].reshape(tensor_n, used_n, feat_loc, rank_n)
    ua_all = tall[:, n_tok_el + n_a_el :].reshape(tensor_n, used_n, feat_loc, rank_n)

    def to_cols(a):
        return jnp.transpose(a, (0, 2, 1, 3)).reshape(tensor_n * feat_loc, used_n * rank_n)

    both_in = jnp.concatenate([to_cols(ga_all), to_cols(ua_all)], axis=1)
    low = jnp.dot(piece, both_in, preferred_element_type=jnp.float32).reshape(
        group_tok, 2, used_n, rank_n
    )
    mid_gate = select_token(low[:, 0], token_weights).astype(jnp.bfloat16)
    mid_up = select_token(low[:, 1], token_weights).astype(jnp.bfloat16)
    weights_bf = token_weights.astype(jnp.bfloat16)

    def spread(mid):
        return (mid[:, None, :] * weights_bf[:, :, None]).reshape(group_tok, used_n * rank_n)

    gate_part = jnp.dot(piece, gate_weight_matrix, preferred_element_type=jnp.float32)
    up_part = jnp.dot(piece, up_weight, preferred_element_type=jnp.float32)
    gate_adapter_rows = jnp.dot(
        spread(mid_gate),
        sel_gb.reshape(used_n * rank_n, hidden_local),
        preferred_element_type=jnp.float32,
    )
    up_adapter_rows = jnp.dot(
        spread(mid_up),
        sel_ub.reshape(used_n * rank_n, hidden_local),
        preferred_element_type=jnp.float32,
    )
    gate_preactivation = gate_part + adapter_scale * gate_adapter_rows
    up_preactivation = up_part + adapter_scale * up_adapter_rows
    hidden = (jax.nn.silu(gate_preactivation) * up_preactivation).astype(jnp.bfloat16)
    down_part = jnp.dot(hidden, w_down, preferred_element_type=jnp.float32).astype(jnp.bfloat16)
    da_cols = jnp.transpose(sel_da, (1, 0, 2)).reshape(hidden_local, used_n * rank_n)
    down_adapter_rows = jnp.dot(hidden, da_cols, preferred_element_type=jnp.float32).reshape(
        group_tok, used_n, rank_n
    )
    partial_down = select_token(down_adapter_rows, token_weights).astype(jnp.bfloat16)
    joined = jnp.concatenate([down_part, partial_down], axis=1)
    reduced = lax.psum_scatter(joined, "tensor", scatter_dimension=0, tiled=True)
    down_total_sum = reduced[:, :d_model].astype(jnp.float32)
    mid_down = reduced[:, d_model:]
    spread_down = (mid_down[:, None, :] * own_weights.astype(jnp.bfloat16)[:, :, None]).reshape(
        tok_dev, used_n * rank_n
    )
    adapter_down_term = jnp.dot(
        spread_down,
        sel_db.reshape(used_n * rank_n, sel_db.shape[2]),
        preferred_element_type=jnp.float32,
    )
    return (residual_float + down_total_sum + adapter_scale * adapter_down_term).astype(
        jnp.bfloat16
    )[None]


def solution(mesh):
    placed = (
        P("seq", "tensor", None),
        P(),
        P(None, "tensor"),
        P(None, "tensor"),
        P("tensor", None),
        P("seq", "tensor", None),
        P("seq", None, "tensor"),
        P("seq", "tensor", None),
        P("seq", None, "tensor"),
        P("seq", "tensor", None),
        P("seq", None, None),
        P("seq", None),
        P("seq", None),
        P(),
        P(),
    )
    return jax.shard_map(
        local, mesh=mesh, in_specs=placed, out_specs=P("seq", "tensor", None), check_vma=False
    )
```

profile of v0, /device:TPU:8, one launch (start us, length us, event | category | flops | bytes accessed | tf_op | source)
XLA Modules:
  0.0 427.2 jit_solution(15833528576533599783)
XLA Ops:
  6.6 1.1 copy.47
  9.9 0.9 reshape.177
  10.8 0.9 reshape.178
  11.7 0.9 concatenate.12
  14.0 91.6 %all-gather.10.cloned.1.call-done = bf16[16,4,18464]{2,1,0:T(4,128)(2,1)} async-done(((bf16[1,4,18464]{2,1,0:T(4,128)(2,1)}), bf16[16,4,18464]{2,1,0:T(4,128)(2,1)}) %all-gather.10.cloned.1.call-update) | async-done | bytes 2363408 | tf_op jit(solution)/shard_map/all_gather | solution.py:54
  105.6 4.3 %reshape.194 = bf16[64,18464]{1,0:T(8,128)(2,1)} reshape(bf16[16,4,18464]{2,1,0:T(4,128)(2,1)} %all-gather.10.cloned.1.call-done) | data formatting | bytes 4726784
  110.0 2.2 convolution_convert_fusion.1
  114.2 1.0 reshape_reshape.17
  115.2 1.0 reshape_reshape.18
  116.2 1.0 reshape.187
  117.2 1.2 copy.52
  118.4 87.7 %all-gather.8.cloned.1.call-done = bf16[2097152]{0:T(1024)(128)(2,1)} async-done(((bf16[65536]{0:T(1024)(128)(2,1)}), bf16[2097152]{0:T(1024)(128)(2,1)}) %all-gather.8.cloned.1.call-update) | async-done | bytes 4194320 | tf_op jit(solution)/shard_map/all_gather | solution.py:83
  206.2 5.5 %reshape.192 = bf16[32,65536]{1,0:T(8,128)(2,1)} reshape(bf16[2097152]{0:T(1024)(128)(2,1)} %all-gather.8.cloned.1.call-done) | data formatting | bytes 8388608 | tf_op jit(solution)/shard_map/all_gather | solution.py:83
  211.7 1.7 slice.50
  213.4 2.4 reshape.195
  215.8 2.4 reshape.180
  218.2 2.7 fusion.23
  221.0 3.1 copy.48
  224.1 4.9 %copy.49 = bf16[32,64,16,16]{1,0,3,2:T(8,128)(2,1)S(1)} copy(bf16[32,64,16,16]{0,3,1,2:T(8,128)(2,1)} %bitcast.93) | data formatting | bytes 2097152 | tf_op jit(solution)/shard_map/transpose | solution.py:91
  228.9 2.4 reshape.182
  231.4 4.6 %copy.50 = bf16[32,16384]{0,1:T(8,128)(2,1)} copy(bf16[32,16384]{1,0:T(8,128)(2,1)} %get-tuple-element.8) | data formatting | bytes 2097152 | tf_op jit(solution)/shard_map/slice | solution.py:88
  236.0 4.9 %copy.51 = bf16[32,64,16,16]{1,0,3,2:T(8,128)(2,1)S(1)} copy(bf16[32,64,16,16]{0,3,1,2:T(8,128)(2,1)} %bitcast.94) | data formatting | bytes 2097152 | tf_op jit(solution)/shard_map/transpose | solution.py:91
  240.8 2.4 reshape.184
  243.3 2.0 pad_maximum_fusion.1
  245.6 1.3 fusion.3
  247.6 0.9 fusion.25
  251.3 1.3 convolution_convert_fusion.2
  252.6 1.6 pad_maximum_fusion
  254.4 40.6 %all-gather.6.cloned.1.call-done = bf16[64,16,2048]{2,1,0:T(8,128)(2,1)} async-done(((bf16[4,16,2048]{2,1,0:T(8,128)(2,1)}), bf16[64,16,2048]{2,1,0:T(8,128)(2,1)}) %all-gather.6.cloned.1.call-update) | async-done | bytes 4194320 | tf_op jit(solution)/shard_map/all_gather | solution.py:64
  295.0 4.6 %copy.61 = bf16[8,8,16,2048]{3,1,2,0:T(8,128)(2,1)S(1)} copy(bf16[8,8,16,2048]{3,2,1,0:T(8,128)(2,1)} %bitcast.97) | data formatting | bytes 8388608
  300.9 117.1 %reduce-scatter.2.cloned.1.call-done = bf16[16,2064]{1,0:T(8,128)(2,1)} async-done(((bf16[512,2064]{1,0:T(8,128)(2,1)}), bf16[16,2064]{1,0:T(8,128)(2,1)}) %reduce-scatter.2.cloned.1.call-update) | async-done | bytes 66064 | tf_op jit(solution)/shard_map/reduce_scatter | solution.py:126
  419.0 1.8 fusion.2
  (77 shorter events, 11.6 us)
Async XLA Ops:
  6.5 244.8 %copy-start = (bf16[342,2048]{1,0:T(8,128)(2,1)S(1)}, bf16[342,2048]{1,0:T(8,128)(2,1)}, u32[]{:S(2)}) copy-start(bf16[342,2048]{1,0:T(8,128)(2,1)} %param.19) | copy-start | bytes 4202500
  6.5 6.9 %copy-start.4 = (bf16[1,16,2048]{2,1,0:T(8,128)(2,1)S(1)}, bf16[1,16,2048]{2,1,0:T(8,128)(2,1)}, u32[]{:S(2)}) copy-start(bf16[1,16,2048]{2,1,0:T(8,128)(2,1)} %param.15) | copy-start | bytes 196612
  6.5 7.3 %copy-start.13 = (s32[16]{0:T(128)S(1)}, s32[16]{0:T(128)}, u32[]{:S(2)}) copy-start(s32[16]{0:T(128)} %param.28) | copy-start | bytes 196
  6.5 7.3 %copy-start.12 = (s32[64]{0:T(128)S(1)}, s32[64]{0:T(128)}, u32[]{:S(2)}) copy-start(s32[64]{0:T(128)} %param.29) | copy-start | bytes 772
  6.5 99.1 %all-gather.10.cloned.1.call-start = ((), (), s32[]{:S(2)}) async-start(), calls=%async_computation.4 | async-start | bytes 2524160 | tf_op jit(solution)/shard_map/all_gather | solution.py:54
  12.7 193.5 %all-gather.8.cloned.1.call-start = ((), (), s32[]{:S(2)}) async-start(), calls=%async_computation.3 | async-start | bytes 4325376 | tf_op jit(solution)/shard_map/all_gather | solution.py:83
  14.0 95.9 %copy-start.7 = (s32[16]{0:T(128)}, s32[16]{0:T(128)S(1)}, u32[]{:S(2)}) copy-start(s32[16]{0:T(128)S(1)} %select_reduce_fusion.1) | copy-start | bytes 196
  109.9 3.7 copy-start.14
  109.9 4.0 copy-start.9
  112.9 182.2 %all-gather.6.cloned.1.call-start = ((), (), s32[]{:S(2)}) async-start(), calls=%async_computation.2 | async-start | bytes 4456448 | tf_op jit(solution)/shard_map/all_gather | solution.py:64
  113.6 304.4 %reduce-scatter.2.cloned.1.call-start = ((), (), s32[]{:S(2)}) async-start(), calls=%async_computation.1 | async-start | bytes 2297856 | tf_op jit(solution)/shard_map/reduce_scatter | solution.py:126
  243.3 2.3 copy-start.2
  245.6 1.6 copy-start.1
  245.6 2.0 copy-start.10
  247.5 0.9 copy-start.3
  247.5 1.5 copy-start.11
  249.0 0.9 copy-start.6
  250.0 0.9 copy-start.5
  295.0 4.6 %copy-start.8 = (s32[16]{0:T(128)S(1)}, s32[16]{0:T(128)}, u32[]{:S(2)}) copy-start(s32[16]{0:T(128)} %copy-done.7) | copy-start | bytes 196
Sparse Core Ops, SparseCore 0:
  12.8 92.7 all-gather.9
  113.0 93.1 all-gather.7
  208.3 86.7 all-gather.5
  299.5 118.5 reduce-scatter.1
where the time goes:
time: 428 us; the launch traced here: 427 us
  waiting for transfers between devices  338 us (79%)
  local copies, waits for them, and re-layouts  59.9 us (14%)
  between operations  13.5 us (3%)
  matrix products  10 us (2%)
  other arithmetic  5.86 us (1%)
    reduce_scatter x1, waiting for transfers between devices, local(): lax.psum_scatter(joined, 'tensor', scatter_dimension=0, tiled=True)  117 us
    all_gather x1, waiting for transfers between devices, local(): whole = lax.all_gather(pack, 'seq', axis=0, tiled=True)  91.6 us
    all_gather x1, waiting for transfers between devices, local(): tall = lax.all_gather(tpack, 'tensor', axis=0, tiled=False)  87.7 us
    all_gather x1, waiting for transfers between devices, local(): whole_db = lax.all_gather(down_b, 'seq', axis=0, tiled=True)  40.6 us
    unnamed x43, local copies, waits for them, and re-layouts  13.5 us
    transpose x2, local copies, waits for them, and re-layouts, to_cols(): jnp.transpose(a, (0, 2, 1, 3)).reshape(tensor_n * feat_loc, used_n * rank_n)  9.76 us
  transfers between devices with their start and end apart: 4, of which 4 were waited for; matrix products, arithmetic and copies ran while one was open for 14% of the time, Pallas kernels for 0%

commit v1 on v0

--- a/solution.py
+++ b/solution.py
@@ -51,7 +51,9 @@
     pieces = (gate_a, up_a, gate_b, up_b, down_a)
     widths = [p.shape[1] * p.shape[2] for p in pieces]
     pack = jnp.concatenate([p.reshape(slots_loc, -1) for p in pieces], axis=1)
-    whole = lax.all_gather(pack, "seq", axis=0, tiled=True)
+    whole = jnp.concatenate(
+        lax.all_to_all(jnp.stack([pack] * lax.axis_size("seq")), "seq", 0, 0), 0
+    )
     chosen = pick_rows(picker, whole)
     offs = [0]
     for w in widths:

time: 428 us -> 402 us (0.939)
  waiting for transfers between devices: 338 us -> 301 us
  starting transfers between devices: 0.15 us -> 10.2 us
    all_gather x1 -> x0, waiting for transfers between devices: 91.6 us -> none  [local(): whole = lax.all_gather(pack, 'seq', axis=0, tiled=True)]
    all_to_all x0 -> x1, waiting for transfers between devices: none -> 44.7 us  [local(): lax.all_to_all(jnp.stack([pack] * lax.axis_size('seq')), 'seq', 0, 0)]
    all_gather x1, waiting for transfers between devices: 87.7 us -> 98 us  [local(): tall = lax.all_gather(tpack, 'tensor', axis=0, tiled=False)]
    all_to_all x0 -> x1, starting transfers between devices: none -> 10.1 us  [local(): lax.all_to_all(jnp.stack([pack] * lax.axis_size('seq')), 'seq', 0, 0)]
    reshape x0 -> x1, local copies, waits for them, and re-layouts: none -> 4.34 us  [local(): jnp.concatenate(lax.all_to_all(jnp.stack([pack] * lax.axis_size('seq')),...]
    unnamed x43 -> x44, local copies, waits for them, and re-layouts: 13.5 us -> 9.2 us
where the time goes in v1:
time: 402 us; the launch traced here: 401 us
  waiting for transfers between devices  301 us (75%)
  local copies, waits for them, and re-layouts  61.3 us (15%)
  between operations  13.5 us (3%)
  starting transfers between devices  10.2 us (3%)
  matrix products  10 us (2%)
  other arithmetic  5.17 us (1%)
    reduce_scatter x1, waiting for transfers between devices, local(): lax.psum_scatter(joined, 'tensor', scatter_dimension=0, tiled=True)  117 us
    all_gather x1, waiting for transfers between devices, local(): tall = lax.all_gather(tpack, 'tensor', axis=0, tiled=False)  98 us
    all_to_all x1, waiting for transfers between devices, local(): lax.all_to_all(jnp.stack([pack] * lax.axis_size('seq')), 'seq', 0, 0)  44.7 us
    all_gather x1, waiting for transfers between devices, local(): whole_db = lax.all_gather(down_b, 'seq', axis=0, tiled=True)  40.5 us
    all_to_all x1, starting transfers between devices, local(): lax.all_to_all(jnp.stack([pack] * lax.axis_size('seq')), 'seq', 0, 0)  10.1 us
    transpose x2, local copies, waits for them, and re-layouts, to_cols(): jnp.transpose(a, (0, 2, 1, 3)).reshape(tensor_n * feat_loc, used_n * rank_n)  9.76 us
    unnamed x44, local copies, waits for them, and re-layouts  9.2 us
  transfers between devices with their start and end apart: 4, of which 4 were waited for; matrix products, arithmetic and copies ran while one was open for 14% of the time, Pallas kernels for 0%

profile of v1, /device:TPU:8, one launch (start us, length us, event | category | flops | bytes accessed | tf_op | source)
XLA Modules:
  0.0 401.4 jit_solution(9721921179251261117)
XLA Ops:
  6.5 1.1 copy.47
  9.8 0.9 reshape.182
  10.7 0.9 reshape.183
  12.0 2.0 stack.2
  14.0 10.1 %all-to-all-start = ((bf16[16,4,18464]{2,1,0:T(4,128)(2,1)}), bf16[16,4,18464]{2,1,0:T(4,128)(2,1)}, u32[]{:S(2)}, u32[]{:S(2)}) async-start(bf16[16,4,18464]{2,1,0:T(4,128)(2,1)} %stack.2), calls=%async_computation | async-start | bytes 4751360 | tf_op jit(solution)/shard_map/all_to_all | solution.py:55
  24.8 44.7 %all-to-all-done = bf16[16,4,18464]{2,1,0:T(4,128)(2,1)} async-done(((bf16[16,4,18464]{2,1,0:T(4,128)(2,1)}), bf16[16,4,18464]{2,1,0:T(4,128)(2,1)}, u32[]{:S(2)}, u32[]{:S(2)}) %all-to-all-start) | async-done | bytes 2363424 | tf_op jit(solution)/shard_map/all_to_all | solution.py:55
  69.6 4.3 %reshape.185 = bf16[64,18464]{1,0:T(8,128)(2,1)} reshape(bf16[16,4,18464]{2,1,0:T(4,128)(2,1)} %all-to-all-done) | data formatting | bytes 4726784 | tf_op jit(solution)/shard_map/reshape | solution.py:54
  73.9 2.2 convolution_convert_fusion.1
  78.2 1.0 reshape_reshape.17
  79.1 1.0 reshape_reshape.18
  80.1 1.0 reshape.193
  81.2 1.2 copy.52
  82.4 98.0 %all-gather.6.cloned.1.call-done = bf16[2097152]{0:T(1024)(128)(2,1)} async-done(((bf16[65536]{0:T(1024)(128)(2,1)}), bf16[2097152]{0:T(1024)(128)(2,1)}) %all-gather.6.cloned.1.call-update) | async-done | bytes 4194320 | tf_op jit(solution)/shard_map/all_gather | solution.py:85
  180.4 5.5 %reshape.198 = bf16[32,65536]{1,0:T(8,128)(2,1)} reshape(bf16[2097152]{0:T(1024)(128)(2,1)} %all-gather.6.cloned.1.call-done) | data formatting | bytes 8388608 | tf_op jit(solution)/shard_map/all_gather | solution.py:85
  185.9 1.7 slice.50
  187.6 2.4 reshape.199
  190.0 2.4 reshape.186
  192.4 2.7 fusion.23
  195.2 3.1 copy.48
  198.3 4.9 %copy.49 = bf16[32,64,16,16]{1,0,3,2:T(8,128)(2,1)S(1)} copy(bf16[32,64,16,16]{0,3,1,2:T(8,128)(2,1)} %bitcast.92) | data formatting | bytes 2097152 | tf_op jit(solution)/shard_map/transpose | solution.py:93
  203.2 2.4 reshape.188
  205.6 4.6 %copy.50 = bf16[32,16384]{0,1:T(8,128)(2,1)} copy(bf16[32,16384]{1,0:T(8,128)(2,1)} %get-tuple-element.8) | data formatting | bytes 2097152 | tf_op jit(solution)/shard_map/slice | solution.py:90
  210.2 4.9 %copy.51 = bf16[32,64,16,16]{1,0,3,2:T(8,128)(2,1)S(1)} copy(bf16[32,64,16,16]{0,3,1,2:T(8,128)(2,1)} %bitcast.93) | data formatting | bytes 2097152 | tf_op jit(solution)/shard_map/transpose | solution.py:93
  215.1 2.4 reshape.190
  217.5 2.0 pad_maximum_fusion.1
  219.8 1.3 fusion.3
  225.6 1.3 convolution_convert_fusion.2
  226.9 1.6 pad_maximum_fusion
  228.6 40.5 %all-gather.4.cloned.1.call-done = bf16[64,16,2048]{2,1,0:T(8,128)(2,1)} async-done(((bf16[4,16,2048]{2,1,0:T(8,128)(2,1)}), bf16[64,16,2048]{2,1,0:T(8,128)(2,1)}) %all-gather.4.cloned.1.call-update) | async-done | bytes 4194320 | tf_op jit(solution)/shard_map/all_gather | solution.py:66
  269.1 4.6 %copy.61 = bf16[8,8,16,2048]{3,1,2,0:T(8,128)(2,1)S(1)} copy(bf16[8,8,16,2048]{3,2,1,0:T(8,128)(2,1)} %bitcast.96) | data formatting | bytes 8388608
  275.0 117.1 %reduce-scatter.2.cloned.1.call-done = bf16[16,2064]{1,0:T(8,128)(2,1)} async-done(((bf16[512,2064]{1,0:T(8,128)(2,1)}), bf16[16,2064]{1,0:T(8,128)(2,1)}) %reduce-scatter.2.cloned.1.call-update) | async-done | bytes 66064 | tf_op jit(solution)/shard_map/reduce_scatter | solution.py:128
  393.1 1.8 fusion.2
  (79 shorter events, 12.1 us)
Async XLA Ops:
  6.5 219.0 %copy-start = (bf16[342,2048]{1,0:T(8,128)(2,1)S(1)}, bf16[342,2048]{1,0:T(8,128)(2,1)}, u32[]{:S(2)}) copy-start(bf16[342,2048]{1,0:T(8,128)(2,1)} %param.19) | copy-start | bytes 4202500
  14.0 10.2 %copy-start.7 = (bf16[2048]{0:T(1024)(128)(2,1)S(1)}, bf16[2048]{0:T(1024)(128)(2,1)}, u32[]{:S(2)}) copy-start(bf16[2048]{0:T(1024)(128)(2,1)} %param.16) | copy-start | bytes 12292
  14.0 10.2 %copy-start.4 = (bf16[1,16,2048]{2,1,0:T(8,128)(2,1)S(1)}, bf16[1,16,2048]{2,1,0:T(8,128)(2,1)}, u32[]{:S(2)}) copy-start(bf16[1,16,2048]{2,1,0:T(8,128)(2,1)} %param.15) | copy-start | bytes 196612
  14.0 10.6 %copy-start.13 = (s32[64]{0:T(128)S(1)}, s32[64]{0:T(128)}, u32[]{:S(2)}) copy-start(s32[64]{0:T(128)} %param.29) | copy-start | bytes 772
  14.0 10.6 %copy-start.14 = (s32[16]{0:T(128)S(1)}, s32[16]{0:T(128)}, u32[]{:S(2)}) copy-start(s32[16]{0:T(128)} %param.28) | copy-start | bytes 196
  14.0 55.5 %all-to-all-start = ((bf16[16,4,18464]{2,1,0:T(4,128)(2,1)}), bf16[16,4,18464]{2,1,0:T(4,128)(2,1)}, u32[]{:S(2)}, u32[]{:S(2)}) async-start(bf16[16,4,18464]{2,1,0:T(4,128)(2,1)} %stack.2), calls=%async_computation | async-start | bytes 4751360 | tf_op jit(solution)/shard_map/all_to_all | solution.py:55
  24.1 156.3 %all-gather.6.cloned.1.call-start = ((), (), s32[]{:S(2)}) async-start(), calls=%async_computation.4 | async-start | bytes 4325376 | tf_op jit(solution)/shard_map/all_gather | solution.py:85
  24.8 49.1 %copy-start.8 = (s32[16]{0:T(128)}, s32[16]{0:T(128)S(1)}, u32[]{:S(2)}) copy-start(s32[16]{0:T(128)S(1)} %select_reduce_fusion.1) | copy-start | bytes 196
  73.9 3.7 copy-start.15
  73.9 4.0 copy-start.10
  76.8 192.3 %all-gather.4.cloned.1.call-start = ((), (), s32[]{:S(2)}) async-start(), calls=%async_computation.3 | async-start | bytes 4456448 | tf_op jit(solution)/shard_map/all_gather | solution.py:66
  77.6 314.6 %reduce-scatter.2.cloned.1.call-start = ((), (), s32[]{:S(2)}) async-start(), calls=%async_computation.2 | async-start | bytes 2297856 | tf_op jit(solution)/shard_map/reduce_scatter | solution.py:128
  217.5 2.3 copy-start.2
  219.8 1.6 copy-start.1
  219.8 2.0 copy-start.11
  221.8 0.9 copy-start.3
  221.8 1.5 copy-start.12
  223.3 0.9 copy-start.6
  224.2 0.9 copy-start.5
  269.1 4.6 %copy-start.9 = (s32[16]{0:T(128)S(1)}, s32[16]{0:T(128)}, u32[]{:S(2)}) copy-start(s32[16]{0:T(128)} %copy-done.8) | copy-start | bytes 196
Sparse Core Ops, SparseCore 0:
  76.9 103.4 all-gather.5
  182.5 86.6 all-gather.3
  273.7 118.3 reduce-scatter.1
